TPU v7x, 256 devices: a whole 4x4x8 slice. The times are simulated.
256 devices in a mesh: seq: 64 (over y, z, core), rep: 4 (over x).
Axes of the slice: x: 4, y: 4, z: 8, core: 2. Of those that a mesh axis runs over, the one named last changes fastest.
Arguments:
- tokens: bfloat16 [64, 4, 2048], P('rep'), may hold values from -6 to 6
- lengths: int32 [64], P('rep'), may hold values from 1 to 8192, as said below
- groups: int32 [64], P('rep'), may hold values from 0 to 3
- cache: bfloat16 [4, 8192, 576], P(None, 'seq'), may hold values from -128 to 128
- attn_gain: float32 [2048], replicated, may hold values from 0.3 to 3
- kv_gain: float32 [512], replicated, may hold values from 0.3 to 3
- w_query: bfloat16 [2048, 3072], P('seq'), may hold values from -0.125 to 0.125
- w_latent: bfloat16 [2048, 576], P('seq'), may hold values from -0.25 to 0.25
- w_expand: bfloat16 [512, 4096], P('seq'), may hold values from -0.25 to 0.25
- w_out: bfloat16 [2048, 2048], P('seq'), may hold values from -0.125 to 0.125
- ffn_gain: float32 [2048], replicated, may hold values from 0.5 to 1.5
- w_router: bfloat16 [2048, 64], replicated, may hold values from -5 to 5
- routes: int32 [64, 4, 6], replicated, may hold values from 0 to 63, all different within a row; in each aligned block of 64 rows (0 to 63, 64 to 127, ..., all dimensions but the last counted through in order) at most 12 rows name the same one
- expert_in: bfloat16 [64, 2, 2048, 1408], P('seq', None, None, 'rep'), may hold values from -0.125 to 0.125
- expert_out: bfloat16 [64, 1408, 2048], P('seq', 'rep'), may hold values from -0.15625 to 0.15625
- shared_in: bfloat16 [2, 2048, 2816], P(None, 'seq', 'rep'), may hold values from -0.125 to 0.125
- shared_out: bfloat16 [2816, 2048], P('rep', 'seq'), may hold values from -0.109375 to 0.109375
Outputs:
- layer_out: bfloat16 [64, 4, 2048], P('rep')
Inputs may be any that keep to these rules, and one draw needn't show every extreme that they name: Request b reads cache rows 0 to lengths[b] - 1 of its group; some request reads all 8192 rows. `routes`: in each aligned block of 64 rows (the tokens of one index of rep) no expert is named by more than 12 rows.
All inputs are finite; a program needn't handle non-finite values.
Results may differ from a plain program's by a relative error of at most 0.018.
The roundings to bfloat16 on the way count: a program that leaves them out, or rounds other values in their place, can miss the bound.
Values may be sent and summed in bfloat16 or wider, within the bound.
No kernel may reach another device: no remote copies, remote signals or barrier semaphores. Data moves between devices by JAX's collectives and lax.ppermute only.
A program may use at most 320 MiB of HBM per device.

v0:
```python
import jax
import jax.numpy as jnp
from jax import lax
from jax.sharding import PartitionSpec as P

D = 2048
H = 16
DN = 128
DR = 64
KVL = 512
TOPK = 6
NTOK = 4


EPS = 1e-06
NEG = -1e30


def rms_scale(value_rows, gain):
    wide = value_rows.astype(jnp.float32)
    return wide * lax.rsqrt(jnp.mean(wide * wide, axis=-1, keepdims=True) + EPS) * gain


def angles(places, half):
    freq = 10000.0 ** (-jnp.arange(half, dtype=jnp.float32) / half)
    return places.astype(jnp.float32)[..., None] * freq


def rotate(value_rows, theta):
    half = value_rows.shape[-1] // 2
    first, second = (value_rows[..., :half], value_rows[..., half:])
    cosine, sine = (jnp.cos(theta), jnp.sin(theta))
    return jnp.concatenate(
        [first * cosine - second * sine, first * sine + second * cosine], axis=-1
    )


def per_device(
    tokens,
    lengths,
    groups,
    cache,
    attn_gain,
    kv_gain,
    w_query,
    w_latent,
    w_expand,
    w_out,
    ffn_gain,
    w_router,
    routes,
    expert_in,
    expert_out,
    shared_in,
    shared_out,
):
    seq_here = lax.axis_index("seq")
    sequence_count = lax.axis_size("seq")
    rep_count = lax.axis_size("rep")
    local_req = tokens.shape[0]
    tok_rows = local_req * NTOK
    head_rows = tok_rows * H
    scale = (DN + DR) ** (-0.5)
    flat = tokens.reshape(tok_rows, D)
    normed = rms_scale(flat, attn_gain).astype(jnp.bfloat16)
    slab = w_query.shape[0]
    own_cols = lax.dynamic_slice_in_dim(normed, seq_here * slab, slab, 1)
    query, latent = lax.psum(
        (
            jnp.dot(own_cols, w_query, preferred_element_type=jnp.float32),
            jnp.dot(own_cols, w_latent, preferred_element_type=jnp.float32),
        ),
        "seq",
    )
    expand = lax.all_gather(w_expand, "seq", axis=0, tiled=True).reshape(KVL, H, 2, DN)
    places = lengths[:, None] + jnp.arange(NTOK, dtype=jnp.int32)[None, :]
    theta = angles(places, DR // 2).reshape(tok_rows, DR // 2)
    query = query.reshape(tok_rows, H, DN + DR)
    q_nope = query[:, :, :DN].astype(jnp.bfloat16)
    q_rope = rotate(query[:, :, DN:], theta[:, None, :]).astype(jnp.bfloat16)
    c_new = rms_scale(latent[:, :KVL], kv_gain).astype(jnp.bfloat16)
    k_rope = rotate(latent[:, KVL:], theta).astype(jnp.bfloat16)
    q_lat = jnp.einsum(
        "rhn,lhn->rhl", q_nope, expand[:, :, 0, :], preferred_element_type=jnp.float32
    ).astype(jnp.bfloat16)
    q_cat = jnp.concatenate([q_lat, q_rope], axis=-1).reshape(head_rows, KVL + DR)
    row_len = jnp.repeat(lengths, NTOK * H)
    row_grp = jnp.repeat(groups, NTOK * H)
    span = cache.shape[1]
    places_here = seq_here * span + jnp.arange(span, dtype=jnp.int32)
    live = places_here[None, :] < row_len[:, None]
    best = jnp.full((head_rows,), NEG, jnp.float32)
    mass = jnp.zeros((head_rows,), jnp.float32)
    acc = jnp.zeros((head_rows, KVL), jnp.float32)
    for group in range(cache.shape[0]):
        keys = cache[group]
        score = jnp.einsum("rc,jc->rj", q_cat, keys, preferred_element_type=jnp.float32) * scale
        mine = row_grp == group
        valid = live & mine[:, None]
        peak = jnp.max(jnp.where(valid, score, NEG), axis=1)
        expo = jnp.where(valid, jnp.exp(score - peak[:, None]), 0.0)
        summed = jnp.dot(
            expo.astype(jnp.bfloat16), keys[:, :KVL], preferred_element_type=jnp.float32
        )
        best = jnp.where(mine, peak, best)
        mass = jnp.where(mine, jnp.sum(expo, axis=1), mass)
        acc = jnp.where(mine[:, None], summed, acc)
    top_all = lax.pmax(best, "seq")
    shrink = jnp.exp(best - top_all)
    mass, acc = lax.psum((mass * shrink, acc * shrink[:, None]), "seq")
    best = top_all
    k_new = jnp.concatenate([c_new, k_rope], axis=-1).reshape(local_req, NTOK, KVL + DR)
    q_four = q_cat.reshape(local_req, NTOK, H, KVL + DR)
    fresh = jnp.einsum("bthc,buc->bthu", q_four, k_new, preferred_element_type=jnp.float32) * scale
    causal = (jnp.arange(NTOK)[:, None] >= jnp.arange(NTOK)[None, :])[None, :, None, :]
    causal_rows = jnp.broadcast_to(causal, (local_req, NTOK, H, NTOK)).reshape(head_rows, NTOK)
    fresh = jnp.where(causal_rows, fresh.reshape(head_rows, NTOK), NEG)
    top = jnp.maximum(best, jnp.max(fresh, axis=1))
    keep = jnp.exp(best - top)
    fresh_w = jnp.where(causal_rows, jnp.exp(fresh - top[:, None]), 0.0)
    mass = mass * keep + jnp.sum(fresh_w, axis=1)
    fresh_sum = jnp.einsum(
        "bthu,bul->bthl",
        fresh_w.astype(jnp.bfloat16).reshape(local_req, NTOK, H, NTOK),
        c_new.reshape(local_req, NTOK, KVL),
        preferred_element_type=jnp.float32,
    ).reshape(head_rows, KVL)
    acc = acc * keep[:, None] + fresh_sum
    o_lat = (acc / mass[:, None]).astype(jnp.bfloat16).reshape(tok_rows, H, KVL)
    value = (
        jnp.einsum("rhl,lhn->rhn", o_lat, expand[:, :, 1, :], preferred_element_type=jnp.float32)
        .astype(jnp.bfloat16)
        .reshape(tok_rows, H * DN)
    )
    out_rows = w_out.shape[0]
    own_value = lax.dynamic_slice_in_dim(value, seq_here * out_rows, out_rows, 1)
    attn = lax.psum(jnp.dot(own_value, w_out, preferred_element_type=jnp.float32), "seq")
    resid = (flat.astype(jnp.float32) + attn).astype(jnp.bfloat16)
    normed2 = rms_scale(resid, ffn_gain).astype(jnp.bfloat16)
    every = lax.all_gather(normed2, "rep", axis=0, tiled=True)
    all_rows = every.shape[0]
    gates = jax.nn.softmax(jnp.dot(every, w_router, preferred_element_type=jnp.float32), axis=-1)
    chosen = routes.reshape(all_rows, TOPK)
    picked = jnp.take_along_axis(gates, chosen, axis=1)
    local_exp = expert_in.shape[0]
    own_expert = seq_here * local_exp
    match = chosen == own_expert
    hit = jnp.any(match, axis=1)
    coef = jnp.sum(jnp.where(match, picked, 0.0), axis=1)
    cap = max(2, min(tok_rows, 2 * tok_rows * TOPK // (local_exp * sequence_count)))
    slots = rep_count * cap
    rank = jnp.cumsum(hit.reshape(rep_count, tok_rows).astype(jnp.int32), axis=1) - 1
    slot_of = (jnp.arange(rep_count, dtype=jnp.int32)[:, None] * cap + rank).reshape(all_rows)
    slot_of = jnp.where(hit, slot_of, -1)
    pick = jnp.arange(slots, dtype=jnp.int32)[:, None] == slot_of[None, :]
    gathered = jnp.dot(pick.astype(jnp.bfloat16), every, preferred_element_type=jnp.float32).astype(
        jnp.bfloat16
    )
    both = jnp.einsum("rd,kdf->krf", gathered, expert_in[0], preferred_element_type=jnp.float32)
    act = (jax.nn.silu(both[0]) * both[1]).astype(jnp.bfloat16)
    expert_y = jnp.dot(act, expert_out[0], preferred_element_type=jnp.float32)
    shared_both = jnp.einsum(
        "rd,kdf->krf",
        every,
        lax.all_gather(shared_in, "seq", axis=1, tiled=True),
        preferred_element_type=jnp.float32,
    )
    shared_act = (jax.nn.silu(shared_both[0]) * shared_both[1]).astype(jnp.bfloat16)
    shared_part = jnp.dot(shared_act, shared_out, preferred_element_type=jnp.float32)
    out_cols = shared_out.shape[1]
    pick_wide = pick.astype(jnp.float32)
    routed = lax.dot_general(
        pick_wide, expert_y, (((0,), (0,)), ((), ())), precision=lax.Precision.HIGHEST
    )
    routed = routed * coef[:, None]
    block = lax.dynamic_slice_in_dim(routed, seq_here * out_cols, out_cols, 1) + shared_part
    mine_rows = lax.psum_scatter(
        lax.dynamic_update_slice_in_dim(routed, block, seq_here * out_cols, 1).astype(jnp.bfloat16),
        "rep",
        scatter_dimension=0,
        tiled=True,
    ).astype(jnp.float32)
    total = lax.psum(mine_rows, "seq")
    return (resid.astype(jnp.float32) + total).astype(jnp.bfloat16).reshape(tokens.shape)


def solution(mesh):
    placed = (
        P("rep", None, None),
        P("rep"),
        P("rep"),
        P(None, "seq", None),
        P(),
        P(),
        P("seq", None),
        P("seq", None),
        P("seq", None),
        P("seq", None),
        P(),
        P(),
        P(),
        P("seq", None, None, "rep"),
        P("seq", "rep", None),
        P(None, "seq", "rep"),
        P("rep", "seq"),
    )
    return jax.shard_map(
        per_device, mesh=mesh, in_specs=placed, out_specs=P("rep", None, None), check_vma=False
    )
```

profile of v0, /device:TPU:4, one launch (start us, length us, event | category | flops | bytes accessed | tf_op | source)
XLA Modules:
  0.0 1220.1 jit_solution(15888302039087194198)
XLA Ops:
  6.5 1.1 reshape.311
  7.7 1.4 multiply_reduce_fusion
  9.2 0.8 dynamic-slice
  9.9 2.1 fusion.110
  12.0 2.6 reshape.301
  14.7 2.8 copy.74
  22.6 0.8 multiply_cosine_fusion
  23.4 0.9 fusion.112
  24.3 1.9 slice_bitcast_fusion.14
  26.2 180.0 %all-reduce.6.cloned.1.call-done = f32[64,16,192]{2,0,1:T(8,128)} async-done(((f32[64,16,192]{2,0,1:T(8,128)}), f32[64,16,192]{2,0,1:T(8,128)}) %all-reduce.6.cloned.1.call-update) | async-done | bytes 786448 | tf_op jit(solution)/shard_map/psum | solution.py:68
  206.2 1.5 subtract_convert_fusion
  207.7 78.3 %all-gather.4.cloned.1.call-done = bf16[512,4096]{1,0:T(8,128)(2,1)} async-done(((bf16[8,4096]{1,0:T(8,128)(2,1)}), bf16[512,4096]{1,0:T(8,128)(2,1)}) %all-gather.4.cloned.1.call-update) | async-done | bytes 4194320 | tf_op jit(solution)/shard_map/all_gather | solution.py:75
  286.0 6.5 copy.75
  292.5 2.2 fusion.10
  294.9 0.7 copy.77
  297.7 2.3 fusion.37
  301.2 127.0 %pmax.7 = f32[1024]{0:T(1024)} all-reduce(f32[1024]{0:T(1024)} %select_select_fusion), channel_id=1, replica_groups=mesh['seq'=64,'rep'=4] {'seq'}, use_global_device_ids=true, to_apply=%region_6.7 | all-reduce | flops 1024 | bytes 8192 | tf_op jit(solution)/shard_map/pmax | solution.py:108
  428.2 1.6 fusion.39
  429.9 1.7 fusion.50
  432.9 2.7 select_multiply_fusion
  435.7 124.4 %psum.45 = f32[1024]{0:T(1024)S(1)} all-reduce(f32[1024]{0:T(1024)S(1)} %get-tuple-element.19), channel_id=1, replica_groups=mesh['seq'=64,'rep'=4] {'seq'}, use_global_device_ids=true, to_apply=%region_15.16 | all-reduce | flops 1024 | bytes 8192 | tf_op jit(solution)/shard_map/psum | solution.py:110
  560.1 59.7 %all-reduce.10.cloned.1.call-done = (f32[64,576]{1,0:T(8,128)}, f32[1024,512]{1,0:T(8,128)}) async-done(((f32[64,576]{1,0:T(8,128)}, f32[1024,512]{1,0:T(8,128)}), (f32[64,576]{1,0:T(8,128)}, f32[1024,512]{1,0:T(8,128)})) %all-reduce.10.cloned.1.call-update) | async-done | bytes 2244624 | tf_op jit(solution)/shard_map/psum | solution.py:68
  619.7 1.0 multiply_reduce_fusion.1
  620.8 1.0 subtract_convert_fusion.1
  621.8 1.0 multiply_convert_fusion
  622.9 3.3 fusion.114
  627.3 1.0 copy-done.9
  628.6 1.8 copy-done.2
  630.5 0.8 fusion.12
  631.4 1.1 fusion.96
  632.5 180.4 %all-reduce.8.cloned.1.call-done = f32[64,2048]{1,0:T(8,128)} async-done(((f32[64,2048]{1,0:T(8,128)}), f32[64,2048]{1,0:T(8,128)}) %all-reduce.8.cloned.1.call-update) | async-done | bytes 524304 | tf_op jit(solution)/shard_map/psum | solution.py:137
  812.9 1.2 fusion.33
  814.8 0.8 fusion.35
  817.8 21.2 %all-gather.6.cloned.1.call-done = bf16[256,2048]{1,0:T(8,128)(2,1)} async-done(((bf16[64,2048]{1,0:T(8,128)(2,1)}), bf16[256,2048]{1,0:T(8,128)(2,1)}) %all-gather.6.cloned.1.call-update) | async-done | bytes 1048592 | tf_op jit(solution)/shard_map/all_gather | solution.py:140
  839.0 1.7 fusion.115
  840.8 12.7 %gather_fusion = f32[1536]{0:T(1024)S(1)} fusion(f32[256,64]{0,1:T(8,128)S(1)} %fusion.87, s32[1536]{0:T(1024)S(1)} %reshape.313), kind=kCustom, calls=%fused_computation | custom fusion | bytes 24576 | tf_op jit(solution)/shard_map/jit(take_along_axis)/gather | solution.py:144
  854.1 2.3 fusion.13
  856.4 1.7 fusion.8
  858.1 2.4 convolution_multiply_fusion
  860.5 64.0 %all-gather.8.cloned.1.call-done = bf16[2,2048,704]{2,1,0:T(8,128)(2,1)} async-done(((bf16[2,32,704]{2,1,0:T(8,128)(2,1)}), bf16[2,2048,704]{2,1,0:T(8,128)(2,1)}) %all-gather.8.cloned.1.call-update) | async-done | bytes 5767184 | tf_op jit(solution)/shard_map/all_gather | solution.py:165
  924.5 5.7 convolution_bitcast_fusion
  930.2 1.3 convolution_add_fusion
  931.5 1.7 dynamic_update_slice.3
  933.2 2.8 convert_element_type.125
  936.0 21.5 %reduce-scatter.2.cloned.1.call-done = bf16[64,2048]{1,0:T(8,128)(2,1)} async-done(((bf16[256,2048]{1,0:T(8,128)(2,1)}), bf16[64,2048]{1,0:T(8,128)(2,1)}) %reduce-scatter.2.cloned.1.call-update) | async-done | bytes 262160 | tf_op jit(solution)/shard_map/reduce_scatter | solution.py:177
  957.5 253.9 %all-reduce.11 = f32[64,2048]{1,0:T(8,128)} all-reduce(bf16[64,2048]{1,0:T(8,128)(2,1)} %reduce-scatter.2.cloned.1.call-done), channel_id=1, replica_groups=mesh['seq'=64,'rep'=4] {'seq'}, use_global_device_ids=true, to_apply=%region_25.26 | all-reduce | flops 131072 | bytes 786432 | tf_op jit(solution)/shard_map/psum | solution.py:183
  1211.4 1.1 fusion.36
  1212.4 0.8 reshape.310
  (177 shorter events, 14.6 us)
Async XLA Ops:
  6.5 847.5 %copy-start = (bf16[1,2,2048,352]{2,3,1,0:T(8,128)(2,1)S(1)}, bf16[1,2,2048,352]{2,3,1,0:T(8,128)(2,1)}, u32[]{:S(2)}) copy-start(bf16[1,2,2048,352]{2,3,1,0:T(8,128)(2,1)} %param.30) | copy-start | bytes 8650756
  6.5 199.7 %all-reduce.6.cloned.1.call-start = ((), (), s32[]{:S(2)}) async-start(), calls=%async_computation.1 | async-start | bytes 2097152 | tf_op jit(solution)/shard_map/psum | solution.py:68
  7.7 15.7 %copy-start.5 = (f32[64,2048]{1,0:T(8,128)}, f32[64,2048]{1,0:T(8,128)S(1)}, u32[]{:S(2)}) copy-start(f32[64,2048]{1,0:T(8,128)S(1)} %reshape.311) | copy-start | bytes 1572868
  12.0 6.3 copy-start.48
  12.0 6.5 copy-start.49
  14.7 8.7 copy-start.21
  17.5 268.5 %all-gather.4.cloned.1.call-start = ((), (), s32[]{:S(2)}) async-start(), calls=%async_computation.2 | async-start | bytes 4259840 | tf_op jit(solution)/shard_map/all_gather | solution.py:75
  18.3 601.4 %all-reduce.10.cloned.1.call-start = ((), (), s32[]{:S(2)}) async-start(), calls=%async_computation.7 | async-start | bytes 4521984 | tf_op jit(solution)/shard_map/psum | solution.py:68
  18.5 4.9 copy-start.41
  22.1 1.3 copy-start.46
  295.7 2.0 copy-start.1
  295.7 1.2 copy-start.15
  295.7 1.2 copy-start.29
  295.7 1.2 copy-start.36
  295.7 1.2 copy-start.38
  296.3 1.4 copy-start.32
  296.3 1.4 copy-start.34
  297.0 3.1 copy-start.3
  297.6 2.4 copy-start.10
  297.7 2.4 copy-start.22
  297.7 2.4 copy-start.24
  428.2 3.3 copy-start.4
  428.2 3.3 copy-start.14
  428.2 3.3 copy-start.16
  428.2 3.3 copy-start.27
  428.2 3.3 copy-start.33
  428.2 3.3 copy-start.39
  429.8 2.4 copy-start.13
  429.8 2.4 copy-start.25
  429.8 2.4 copy-start.30
  431.6 1.2 copy-start.19
  431.6 1.2 copy-start.11
  431.6 1.2 copy-start.23
  435.6 185.2 %copy-start.42 = (f32[64]{0:T(128)S(1)}, f32[64]{0:T(128)}, u32[]{:S(2)}) copy-start(f32[64]{0:T(128)} %copy-done.41) | copy-start | bytes 772
  435.6 185.2 %copy-start.47 = (f32[32]{0:T(128)S(1)}, f32[32]{0:T(128)}, u32[]{:S(2)}) copy-start(f32[32]{0:T(128)} %copy-done.46) | copy-start | bytes 388
  435.6 186.2 %copy-start.45 = (f32[512]{0:T(512)S(1)}, f32[512]{0:T(512)}, u32[]{:S(2)}) copy-start(f32[512]{0:T(512)} %param.22) | copy-start | bytes 6148
  435.6 190.7 %copy-start.20 = (f32[1024]{0:T(1024)S(1)}, f32[1024]{0:T(1024)}, u32[]{:S(2)}) copy-start(f32[1024]{0:T(1024)} %pmax.7) | copy-start | bytes 12292
  435.6 377.3 %all-reduce.8.cloned.1.call-start = ((), (), s32[]{:S(2)}) async-start(), calls=%async_computation.3 | async-start | bytes 1048576 | tf_op jit(solution)/shard_map/psum | solution.py:137
  626.7 1.6 copy-start.9
  628.3 2.2 copy-start.2
  630.5 182.5 %copy-start.6 = (f32[64,2048]{1,0:T(8,128)S(1)}, f32[64,2048]{1,0:T(8,128)}, u32[]{:S(2)}) copy-start(f32[64,2048]{1,0:T(8,128)} %copy-done.5) | copy-start | bytes 1572868
  631.3 183.6 %copy-start.40 = (f32[2048]{0:T(1024)S(1)}, f32[2048]{0:T(1024)}, u32[]{:S(2)}) copy-start(f32[2048]{0:T(1024)} %param.27) | copy-start | bytes 24580
  631.3 185.0 %copy-start.18 = (s32[64,4,6]{0,1,2:T(4,128)S(1)}, s32[64,4,6]{0,1,2:T(4,128)}, u32[]{:S(2)}) copy-start(s32[64,4,6]{0,1,2:T(4,128)} %param.29) | copy-start | bytes 18436
  632.5 206.5 %all-gather.6.cloned.1.call-start = ((), (), s32[]{:S(2)}) async-start(), calls=%async_computation.4 | async-start | bytes 1310720 | tf_op jit(solution)/shard_map/all_gather | solution.py:140
  815.7 108.8 %all-gather.8.cloned.1.call-start = ((), (), s32[]{:S(2)}) async-start(), calls=%async_computation.5 | async-start | bytes 6389760 | tf_op jit(solution)/shard_map/all_gather | solution.py:165
  816.3 141.2 %reduce-scatter.2.cloned.1.call-start = ((), (), s32[]{:S(2)}) async-start(), calls=%async_computation.6 | async-start | bytes 1310720 | tf_op jit(solution)/shard_map/reduce_scatter | solution.py:177
  860.5 69.7 %copy-start.50 = (bf16[704,32]{0,1:T(8,128)(2,1)S(1)}, bf16[704,32]{0,1:T(8,128)(2,1)}, u32[]{:S(2)}) copy-start(bf16[704,32]{0,1:T(8,128)(2,1)} %param.33) | copy-start | bytes 135172
  933.2 278.1 %copy-start.8 = (bf16[64,2048]{1,0:T(8,128)(2,1)S(1)}, bf16[64,2048]{1,0:T(8,128)(2,1)}, u32[]{:S(2)}) copy-start(bf16[64,2048]{1,0:T(8,128)(2,1)} %copy-done.7) | copy-start | bytes 786436
  (10 other events, 9.9 us)
Sparse Core Ops, SparseCore 0:
  17.6 188.5 all-reduce.5
  209.4 76.5 all-gather.3
  435.7 183.9 all-reduce.9
  632.6 180.2 all-reduce.7
  815.8 23.1 all-gather.5
  842.0 82.4 all-gather.7
  936.1 21.3 reduce-scatter.1
where the time goes:
time: 1220 us
  waiting for transfers between devices  606 us (50%)
  blocking collectives  505 us (41%)
  local copies, waits for them, and re-layouts  41.6 us (3%)
  matrix products  35.7 us (3%)
  other arithmetic  16.7 us (1%)
  between operations  14.3 us (1%)
    psum x1, blocking collectives, per_device(): total = lax.psum(mine_rows, 'seq')  254 us
    psum x2, waiting for transfers between devices, per_device(): lax.psum((jnp.dot(own_cols, w_query, preferred_element_type=jnp.float32),...  240 us
    psum x1, waiting for transfers between devices, per_device(): lax.psum(jnp.dot(own_value, w_out, preferred_element_type=jnp.float32), '...  180 us
    pmax x1, blocking collectives, per_device(): top_all = lax.pmax(best, 'seq')  127 us
    psum x1, blocking collectives, per_device(): mass, acc = lax.psum((mass * shrink, acc * shrink[:, None]), 'seq')  124 us
    all_gather x1, waiting for transfers between devices, per_device(): lax.all_gather(w_expand, 'seq', axis=0, tiled=True).reshape(KVL, H, 2, DN)  78.3 us
    all_gather x1, waiting for transfers between devices, per_device(): lax.all_gather(shared_in, 'seq', axis=1, tiled=True)  64 us
  transfers between devices with their start and end apart: 7, of which 7 were waited for; matrix products, arithmetic and copies ran while one was open for 3% of the time, Pallas kernels for 0%

commit v1 on v0

v1 whole, which is shorter than its diff:
```python
import jax
import jax.numpy as jnp
from jax import lax
from jax.sharding import PartitionSpec as P

D = 2048
H = 16
DN = 128
DR = 64
KVL = 512
TOPK = 6
NTOK = 4


EPS = 1e-06
NEG = -1e30


def rms_scale(value_rows, gain):
    wide = value_rows.astype(jnp.float32)
    return wide * lax.rsqrt(jnp.mean(wide * wide, axis=-1, keepdims=True) + EPS) * gain


def angles(places, half):
    freq = 10000.0 ** (-jnp.arange(half, dtype=jnp.float32) / half)
    return places.astype(jnp.float32)[..., None] * freq


def rotate(value_rows, theta):
    half = value_rows.shape[-1] // 2
    first, second = (value_rows[..., :half], value_rows[..., half:])
    cosine, sine = (jnp.cos(theta), jnp.sin(theta))
    return jnp.concatenate(
        [first * cosine - second * sine, first * sine + second * cosine], axis=-1
    )


def scatter_rows(x, axis):
    return lax.all_to_all(x, axis, 0, 0, tiled=True)


def sum_to_owner(x, axis, n):
    got = scatter_rows(x, axis)
    return got.reshape((n, got.shape[0] // n) + got.shape[1:]).astype(jnp.float32).sum(0)


def gather_rows(x, axis, n):
    copies = jnp.broadcast_to(x[None], (n,) + x.shape).reshape((n * x.shape[0],) + x.shape[1:])
    return scatter_rows(copies, axis)


def per_device(
    tokens,
    lengths,
    groups,
    cache,
    attn_gain,
    kv_gain,
    w_query,
    w_latent,
    w_expand,
    w_out,
    ffn_gain,
    w_router,
    routes,
    expert_in,
    expert_out,
    shared_in,
    shared_out,
):
    me = lax.axis_index("seq")
    n = lax.axis_size("seq")
    rep_count = lax.axis_size("rep")
    local_req = tokens.shape[0]
    tok_rows = local_req * NTOK
    head_rows = tok_rows * H
    own = tok_rows // n
    scale = (DN + DR) ** (-0.5)
    flat = tokens.reshape(tok_rows, D)
    expand = lax.all_gather(w_expand, "seq", axis=0, tiled=True).reshape(KVL, H, 2, DN)
    shared_full = lax.all_gather(shared_in, "seq", axis=1, tiled=True)

    normed = rms_scale(flat, attn_gain).astype(jnp.bfloat16)
    slab = w_query.shape[0]
    own_cols = lax.dynamic_slice_in_dim(normed, me * slab, slab, 1)
    part = jnp.concatenate(
        [
            jnp.dot(own_cols, w_query, preferred_element_type=jnp.float32),
            jnp.dot(own_cols, w_latent, preferred_element_type=jnp.float32),
        ],
        axis=1,
    )
    mine = sum_to_owner(part, "seq", n)
    qw = H * (DN + DR)
    rows_idx = me * own + jnp.arange(own, dtype=jnp.int32)
    places = lengths[rows_idx // NTOK] + rows_idx % NTOK
    theta = angles(places, DR // 2)
    query = mine[:, :qw].reshape(own, H, DN + DR)
    latent = mine[:, qw:]
    q_nope = query[:, :, :DN].astype(jnp.bfloat16)
    q_rope = rotate(query[:, :, DN:], theta[:, None, :]).astype(jnp.bfloat16)
    c_new = rms_scale(latent[:, :KVL], kv_gain).astype(jnp.bfloat16)
    k_rope = rotate(latent[:, KVL:], theta).astype(jnp.bfloat16)
    pack = jnp.concatenate(
        [q_nope.reshape(own, H * DN), q_rope.reshape(own, H * DR), c_new, k_rope], axis=1
    )
    every_pack = gather_rows(pack, "seq", n)
    q_nope_all = every_pack[:, : H * DN].reshape(tok_rows, H, DN)
    q_rope_all = every_pack[:, H * DN : H * (DN + DR)].reshape(tok_rows, H, DR)
    k_new_all = every_pack[:, H * (DN + DR) :]
    q_lat = jnp.einsum(
        "rhn,lhn->rhl", q_nope_all, expand[:, :, 0, :], preferred_element_type=jnp.float32
    ).astype(jnp.bfloat16)
    q_cat = jnp.concatenate([q_lat, q_rope_all], axis=-1)
    q_rows = q_cat.reshape(head_rows, KVL + DR)

    row_len = jnp.repeat(lengths, NTOK * H)
    row_grp = jnp.repeat(groups, NTOK * H)
    span = cache.shape[1]
    places_here = me * span + jnp.arange(span, dtype=jnp.int32)
    live = places_here[None, :] < row_len[:, None]
    best = jnp.full((head_rows,), NEG, jnp.float32)
    mass = jnp.zeros((head_rows,), jnp.float32)
    acc = jnp.zeros((head_rows, KVL), jnp.float32)
    for group in range(cache.shape[0]):
        keys = cache[group]
        score = jnp.einsum("rc,jc->rj", q_rows, keys, preferred_element_type=jnp.float32) * scale
        hit = row_grp == group
        valid = live & hit[:, None]
        peak = jnp.max(jnp.where(valid, score, NEG), axis=1)
        expo = jnp.where(valid, jnp.exp(score - peak[:, None]), 0.0)
        summed = jnp.dot(
            expo.astype(jnp.bfloat16), keys[:, :KVL], preferred_element_type=jnp.float32
        )
        best = jnp.where(hit, peak, best)
        mass = jnp.where(hit, jnp.sum(expo, axis=1), mass)
        acc = jnp.where(hit[:, None], summed, acc)

    stats = jnp.concatenate([acc, best[:, None], mass[:, None]], axis=1)
    got = scatter_rows(stats, "seq").reshape(n, own * H, KVL + 2)
    peaks = got[:, :, KVL]
    masses = got[:, :, KVL + 1]
    cached_top = jnp.max(peaks, axis=0)
    q_own = lax.dynamic_slice_in_dim(q_cat, me * own, own, 0)
    k_req = k_new_all.reshape(local_req, NTOK, KVL + DR)[rows_idx // NTOK]
    fresh = jnp.einsum("khc,kuc->khu", q_own, k_req, preferred_element_type=jnp.float32) * scale
    causal = (jnp.arange(NTOK)[None, :] <= (rows_idx % NTOK)[:, None])[:, None, :]
    fresh = jnp.where(causal, fresh, NEG).reshape(own * H, NTOK)
    causal_rows = jnp.broadcast_to(causal, (own, H, NTOK)).reshape(own * H, NTOK)
    top = jnp.maximum(cached_top, jnp.max(fresh, axis=1))
    keep = jnp.exp(peaks - top[None, :])
    fresh_w = jnp.where(causal_rows, jnp.exp(fresh - top[:, None]), 0.0)
    total_mass = jnp.sum(masses * keep, axis=0) + jnp.sum(fresh_w, axis=1)
    fresh_sum = jnp.einsum(
        "khu,kul->khl",
        fresh_w.astype(jnp.bfloat16).reshape(own, H, NTOK),
        k_req[:, :, :KVL],
        preferred_element_type=jnp.float32,
    ).reshape(own * H, KVL)
    total_acc = jnp.sum(got[:, :, :KVL] * keep[:, :, None], axis=0) + fresh_sum
    o_lat = (total_acc / total_mass[:, None]).astype(jnp.bfloat16).reshape(own, H, KVL)
    value = (
        jnp.einsum("khl,lhn->khn", o_lat, expand[:, :, 1, :], preferred_element_type=jnp.float32)
        .astype(jnp.bfloat16)
        .reshape(own, H * DN)
    )

    out_rows = w_out.shape[0]
    cols = value.reshape(own, n, out_rows).transpose(1, 0, 2).reshape(n * own, out_rows)
    value_cols = scatter_rows(cols, "seq")
    attn_part = jnp.dot(value_cols, w_out, preferred_element_type=jnp.float32)
    attn = sum_to_owner(attn_part, "seq", n)
    flat_own = lax.dynamic_slice_in_dim(flat, me * own, own, 0)
    resid_own = (flat_own.astype(jnp.float32) + attn).astype(jnp.bfloat16)
    normed2_own = rms_scale(resid_own, ffn_gain).astype(jnp.bfloat16)
    normed2 = gather_rows(normed2_own, "seq", n)

    every = lax.all_gather(normed2, "rep", axis=0, tiled=True)
    all_rows = every.shape[0]
    gates = jax.nn.softmax(jnp.dot(every, w_router, preferred_element_type=jnp.float32), axis=-1)
    chosen = routes.reshape(all_rows, TOPK)
    picked = jnp.take_along_axis(gates, chosen, axis=1)
    local_exp = expert_in.shape[0]
    own_expert = me * local_exp
    match = chosen == own_expert
    used = jnp.any(match, axis=1)
    coef = jnp.sum(jnp.where(match, picked, 0.0), axis=1)
    cap = max(2, min(tok_rows, 2 * tok_rows * TOPK // (local_exp * n)))
    slots = rep_count * cap
    rank = jnp.cumsum(used.reshape(rep_count, tok_rows).astype(jnp.int32), axis=1) - 1
    slot_of = (jnp.arange(rep_count, dtype=jnp.int32)[:, None] * cap + rank).reshape(all_rows)
    slot_of = jnp.where(used, slot_of, -1)
    pick = jnp.arange(slots, dtype=jnp.int32)[:, None] == slot_of[None, :]
    gathered = jnp.dot(pick.astype(jnp.bfloat16), every, preferred_element_type=jnp.float32).astype(
        jnp.bfloat16
    )
    both = jnp.einsum("rd,kdf->krf", gathered, expert_in[0], preferred_element_type=jnp.float32)
    act = (jax.nn.silu(both[0]) * both[1]).astype(jnp.bfloat16)
    expert_y = jnp.dot(act, expert_out[0], preferred_element_type=jnp.float32)
    shared_both = jnp.einsum(
        "rd,kdf->krf", every, shared_full, preferred_element_type=jnp.float32
    )
    shared_act = (jax.nn.silu(shared_both[0]) * shared_both[1]).astype(jnp.bfloat16)
    shared_part = jnp.dot(shared_act, shared_out, preferred_element_type=jnp.float32)
    out_cols = shared_out.shape[1]
    pick_wide = pick.astype(jnp.float32)
    routed = lax.dot_general(
        pick_wide, expert_y, (((0,), (0,)), ((), ())), precision=lax.Precision.HIGHEST
    )
    routed = routed * coef[:, None]
    block = lax.dynamic_slice_in_dim(routed, me * out_cols, out_cols, 1) + shared_part
    mine_rows = lax.psum_scatter(
        lax.dynamic_update_slice_in_dim(routed, block, me * out_cols, 1).astype(jnp.bfloat16),
        "rep",
        scatter_dimension=0,
        tiled=True,
    )
    total = sum_to_owner(mine_rows, "seq", n)
    out_own = (resid_own.astype(jnp.float32) + total).astype(jnp.bfloat16)
    return gather_rows(out_own, "seq", n).reshape(tokens.shape)


def solution(mesh):
    placed = (
        P("rep", None, None),
        P("rep"),
        P("rep"),
        P(None, "seq", None),
        P(),
        P(),
        P("seq", None),
        P("seq", None),
        P("seq", None),
        P("seq", None),
        P(),
        P(),
        P(),
        P("seq", None, None, "rep"),
        P("seq", "rep", None),
        P(None, "seq", "rep"),
        P("rep", "seq"),
    )
    return jax.shard_map(
        per_device, mesh=mesh, in_specs=placed, out_specs=P("rep", None, None), check_vma=False
    )
```

time: 1220 us -> 501 us (0.41)
  waiting for transfers between devices: 606 us -> 206 us
  blocking collectives: 505 us -> 108 us
  starting transfers between devices: 0.25 us -> 25.4 us
  local copies, waits for them, and re-layouts: 41.6 us -> 65.3 us
  other arithmetic: 16.7 us -> 34.2 us
    psum x3 -> x0, waiting for transfers between devices: 420 us -> none  [the longest x2 240 us: per_device(): lax.psum((jnp.dot(own_cols, w_query, preferred_element_type=jnp.float32),...]
    psum x2 -> x0, blocking collectives: 378 us -> none  [the longest x1 254 us: per_device(): total = lax.psum(mine_rows, 'seq')]
    pmax x1 -> x0, blocking collectives: 127 us -> none  [per_device(): top_all = lax.pmax(best, 'seq')]
    all_to_all x0 -> x5, blocking collectives: none -> 108 us  [scatter_rows(): return lax.all_to_all(x, axis, 0, 0, tiled=True)]
    all_to_all x0 -> x3, waiting for transfers between devices: none -> 99.3 us  [scatter_rows(): return lax.all_to_all(x, axis, 0, 0, tiled=True)]
    all_gather x1, waiting for transfers between devices: 78.3 us -> 0.01 us  [per_device(): lax.all_gather(w_expand, 'seq', axis=0, tiled=True).reshape(KVL, H, 2, DN)]
    all_to_all x0 -> x3, starting transfers between devices: none -> 25.3 us  [scatter_rows(): return lax.all_to_all(x, axis, 0, 0, tiled=True)]
  transfers between devices with their start and end apart: 7 -> 7, of which waited for: 7 -> 6; matrix products, arithmetic and copies ran while one was open for 3% -> 11% of each run, Pallas kernels for 0% -> 0%
where the time goes in v1:
time: 501 us; the launch traced here: 496 us
  waiting for transfers between devices  206 us (41%)
  blocking collectives  108 us (22%)
  local copies, waits for them, and re-layouts  65.3 us (13%)
  matrix products  40.8 us (8%)
  other arithmetic  34.2 us (7%)
  starting transfers between devices  25.4 us (5%)
  between operations  16.3 us (3%)
    all_to_all x5, blocking collectives, scatter_rows(): return lax.all_to_all(x, axis, 0, 0, tiled=True)  108 us
    all_to_all x3, waiting for transfers between devices, scatter_rows(): return lax.all_to_all(x, axis, 0, 0, tiled=True)  99.3 us
    all_gather x1, waiting for transfers between devices, per_device(): shared_full = lax.all_gather(shared_in, 'seq', axis=1, tiled=True)  63.8 us
    all_to_all x3, starting transfers between devices, scatter_rows(): return lax.all_to_all(x, axis, 0, 0, tiled=True)  25.3 us
    reduce_scatter x1, waiting for transfers between devices, per_device(): lax.psum_scatter(lax.dynamic_update_slice_in_dim(routed, block, me * out_...  21.5 us
    all_gather x1, waiting for transfers between devices, per_device(): every = lax.all_gather(normed2, 'rep', axis=0, tiled=True)  20.3 us
    unnamed x94, local copies, waits for them, and re-layouts  15.2 us
    gather x5, local copies, waits for them, and re-layouts, per_device(): picked = jnp.take_along_axis(gates, chosen, axis=1)  13.3 us
  transfers between devices with their start and end apart: 7, of which 6 were waited for; matrix products, arithmetic and copies ran while one was open for 11% of the time, Pallas kernels for 0%

profile of v1, /device:TPU:4, one launch (start us, length us, event | category | flops | bytes accessed | tf_op | source)
XLA Modules:
  0.0 495.8 jit_solution(4279647986252005596)
XLA Ops:
  12.9 2.0 copy.151
  14.9 12.3 %all-to-all-start = ((f32[64,1,3648]{2,1,0:T(1,128)}), f32[64,1,3648]{2,1,0:T(1,128)}, u32[]{:S(2)}, u32[]{:S(2)}) async-start(f32[64,1,3648]{2,1,0:T(1,128)} %copy.151), calls=%async_computation | async-start | bytes 1900544 | tf_op jit(solution)/shard_map/all_to_all | solution.py:39
  28.5 26.8 %all-to-all-done = f32[64,1,3648]{2,1,0:T(1,128)} async-done(((f32[64,1,3648]{2,1,0:T(1,128)}), f32[64,1,3648]{2,1,0:T(1,128)}, u32[]{:S(2)}, u32[]{:S(2)}) %all-to-all-start) | async-done | bytes 933920 | tf_op jit(solution)/shard_map/all_to_all | solution.py:39
  55.3 1.8 reduce_sum.150
  61.2 4.6 reduce.25
  67.0 6.7 %all-to-all-start.1 = ((bf16[64,2,1824]{2,1,0:T(2,128)(2,1)}), bf16[64,2,1824]{2,1,0:T(2,128)(2,1)S(1)}, u32[]{:S(2)}, u32[]{:S(2)}) async-start(bf16[64,2,1824]{2,1,0:T(2,128)(2,1)} %reshape.729), calls=%async_computation.1 | async-start | bytes 983040 | tf_op jit(solution)/shard_map/all_to_all | solution.py:39
  79.8 2.1 slice_bitcast_fusion.11
  81.8 13.3 %all-to-all-done.1 = bf16[64,2,1824]{2,1,0:T(2,128)(2,1)S(1)} async-done(((bf16[64,2,1824]{2,1,0:T(2,128)(2,1)}), bf16[64,2,1824]{2,1,0:T(2,128)(2,1)S(1)}, u32[]{:S(2)}, u32[]{:S(2)}) %all-to-all-start.1) | async-done | bytes 466976 | tf_op jit(solution)/shard_map/all_to_all | solution.py:39
  95.1 2.0 reshape.730
  99.3 6.5 %copy.152 = bf16[512,4096]{0,1:T(8,128)(2,1)} copy(bf16[512,4096]{1,0:T(8,128)(2,1)} %all-gather.5.cloned.1.call-done) | data formatting | bytes 8388608 | tf_op jit(solution)/shard_map/all_gather | solution.py:80
  105.7 2.1 fusion.9
  112.5 4.0 fusion.37
  117.9 2.0 fusion.39
  119.9 3.1 fusion.50
  123.0 1.9 fusion.48
  125.0 1.9 fusion.46
  129.2 2.0 copy.157
  131.3 4.3 select_select_fusion
  135.6 1.9 pad_maximum_fusion
  137.5 6.2 %all-to-all-start.2 = ((f32[64,16,514]{2,1,0:T(8,128)}), f32[64,16,514]{2,1,0:T(8,128)}, u32[]{:S(2)}, u32[]{:S(2)}) async-start(f32[64,16,514]{2,1,0:T(8,128)} %pad_maximum_fusion), calls=%async_computation.2 | async-start | bytes 5242880 | tf_op jit(solution)/shard_map/all_to_all | solution.py:39
  146.1 59.3 %all-to-all-done.2 = f32[64,16,514]{2,1,0:T(8,128)} async-done(((f32[64,16,514]{2,1,0:T(8,128)}), f32[64,16,514]{2,1,0:T(8,128)}, u32[]{:S(2)}, u32[]{:S(2)}) %all-to-all-start.2) | async-done | bytes 2105376 | tf_op jit(solution)/shard_map/all_to_all | solution.py:39
  205.4 2.4 fusion.125
  209.8 1.8 fusion.4
  212.6 2.2 fusion.3
  214.9 27.9 %all_to_all.70 = bf16[64,1,32]{2,1,0:T(2,128)(2,1)S(1)} all-to-all(bf16[64,1,32]{2,1,0:T(2,128)(2,1)S(1)} %all_to_all.61), channel_id=1, replica_groups=mesh['seq'=64,'rep'=4] {'seq'}, dimensions={0} | all-to-all | bytes 8192 | tf_op jit(solution)/shard_map/all_to_all | solution.py:39
  243.7 21.0 %all_to_all.71 = f32[64,1,2048]{2,1,0:T(1,128)S(1)} all-to-all(f32[64,1,2048]{2,1,0:T(1,128)S(1)} %copy.166), channel_id=1, replica_groups=mesh['seq'=64,'rep'=4] {'seq'}, dimensions={0} | all-to-all | bytes 1048576 | tf_op jit(solution)/shard_map/all_to_all | solution.py:39
  267.4 2.9 reduce.26
  271.5 18.3 %all_to_all.72 = bf16[64,2,1024]{2,1,0:T(2,128)(2,1)} all-to-all(bf16[64,2,1024]{2,1,0:T(2,128)(2,1)S(1)} %reshape.731), channel_id=1, replica_groups=mesh['seq'=64,'rep'=4] {'seq'}, dimensions={0} | all-to-all | bytes 524288 | tf_op jit(solution)/shard_map/all_to_all | solution.py:39
  289.8 2.1 reshape.732
  295.1 20.3 %all-gather.9.cloned.1.call-done = bf16[256,1,2048]{2,0,1:T(8,128)(2,1)} async-done(((bf16[64,1,2048]{2,0,1:T(8,128)(2,1)}), bf16[256,1,2048]{2,0,1:T(8,128)(2,1)}) %all-gather.9.cloned.1.call-update) | async-done | bytes 1048592 | tf_op jit(solution)/shard_map/all_gather | solution.py:178
  315.4 1.7 fusion.127
  317.2 12.7 %gather_fusion = f32[1536]{0:T(1024)S(1)} fusion(f32[256,64]{0,1:T(8,128)S(1)} %fusion.80, s32[1536]{0:T(1024)S(1)} %reshape.706), kind=kCustom, calls=%fused_computation | custom fusion | bytes 24576 | tf_op jit(solution)/shard_map/jit(take_along_axis)/gather | solution.py:182
  330.5 2.3 fusion.10
  332.8 1.7 fusion.7
  334.5 2.4 convolution_multiply_fusion
  336.9 63.8 %all-gather.7.cloned.1.call-done = bf16[2,2048,704]{2,1,0:T(8,128)(2,1)} async-done(((bf16[2,32,704]{2,1,0:T(8,128)(2,1)}), bf16[2,2048,704]{2,1,0:T(8,128)(2,1)}) %all-gather.7.cloned.1.call-update) | async-done | bytes 5767184 | tf_op jit(solution)/shard_map/all_gather | solution.py:81
  400.7 5.7 %convolution_bitcast_fusion.1 = f32[2,256,704]{1,2,0:T(8,128)S(1)} fusion(bf16[2,2048,704]{2,1,0:T(8,128)(2,1)} %all-gather.7.cloned.1.call-done, bf16[256,1,2048]{2,0,1:T(8,128)(2,1)} %all-gather.9.cloned.1.call-done), kind=kOutput, calls=%fused_computation.16 | convolution fusion | flops 1476395008 | bytes 8257536 | tf_op jit(solution)/shard_map/rd,kdf->krf/dot_general | solution.py:200
  407.7 1.7 dynamic_update_slice.3
  409.4 2.7 convert_element_type.144
  412.2 21.5 %reduce-scatter.2.cloned.1.call-done = bf16[64,2048]{1,0:T(8,128)(2,1)} async-done(((bf16[256,2048]{1,0:T(8,128)(2,1)}), bf16[64,2048]{1,0:T(8,128)(2,1)}) %reduce-scatter.2.cloned.1.call-update) | async-done | bytes 262160 | tf_op jit(solution)/shard_map/reduce_scatter | solution.py:212
  433.7 1.8 reduce.27
  435.6 22.4 %all_to_all.73 = bf16[64,2,1024]{2,1,0:T(2,128)(2,1)} all-to-all(bf16[64,2,1024]{2,1,0:T(2,128)(2,1)S(1)} %reshape.733), channel_id=1, replica_groups=mesh['seq'=64,'rep'=4] {'seq'}, dimensions={0} | all-to-all | bytes 524288 | tf_op jit(solution)/shard_map/all_to_all | solution.py:39
  458.0 2.1 reshape.734
  461.0 2.9 reduce.28
  465.0 17.9 %all_to_all.74 = bf16[64,2,1024]{2,1,0:T(2,128)(2,1)} all-to-all(bf16[64,2,1024]{2,1,0:T(2,128)(2,1)S(1)} %reshape.735), channel_id=1, replica_groups=mesh['seq'=64,'rep'=4] {'seq'}, dimensions={0} | all-to-all | bytes 524288 | tf_op jit(solution)/shard_map/all_to_all | solution.py:39
  482.9 2.1 reshape.736
  485.1 2.2 reduce.19
  487.3 1.8 reshape.662
  (208 shorter events, 44.4 us)
Async XLA Ops:
  6.5 323.9 %copy-start = (bf16[1,2,2048,352]{2,3,1,0:T(8,128)(2,1)S(1)}, bf16[1,2,2048,352]{2,3,1,0:T(8,128)(2,1)}, u32[]{:S(2)}) copy-start(bf16[1,2,2048,352]{2,3,1,0:T(8,128)(2,1)} %param.30) | copy-start | bytes 8650756
  6.5 92.7 %all-gather.5.cloned.1.call-start = ((), (), s32[]{:S(2)}) async-start(), calls=%async_computation.9 | async-start | bytes 4259840 | tf_op jit(solution)/shard_map/all_gather | solution.py:80
  8.4 6.4 %copy-start.10 = (bf16[64,2048]{1,0:T(8,128)(2,1)}, bf16[64,2048]{1,0:T(8,128)(2,1)S(1)}, u32[]{:S(2)}) copy-start(bf16[64,2048]{1,0:T(8,128)(2,1)S(1)} %reshape.648) | copy-start | bytes 786436
  12.9 14.4 %copy-start.38 = (s32[16]{0:T(128)S(1)}, s32[16]{0:T(128)}, u32[]{:S(2)}) copy-start(s32[16]{0:T(128)} %param.18) | copy-start | bytes 196
  12.9 46.1 %copy-start.36 = (f32[512]{0:T(512)S(1)}, f32[512]{0:T(512)}, u32[]{:S(2)}) copy-start(f32[512]{0:T(512)} %param.22) | copy-start | bytes 6148
  14.9 40.5 %all-to-all-start = ((f32[64,1,3648]{2,1,0:T(1,128)}), f32[64,1,3648]{2,1,0:T(1,128)}, u32[]{:S(2)}, u32[]{:S(2)}) async-start(f32[64,1,3648]{2,1,0:T(1,128)} %copy.151), calls=%async_computation | async-start | bytes 1900544 | tf_op jit(solution)/shard_map/all_to_all | solution.py:39
  59.2 14.6 %copy-start.37 = (s32[16]{0:T(128)S(1)}, s32[16]{0:T(128)}, u32[]{:S(2)}) copy-start(s32[16]{0:T(128)} %param.19) | copy-start | bytes 196
  67.0 28.1 %all-to-all-start.1 = ((bf16[64,2,1824]{2,1,0:T(2,128)(2,1)}), bf16[64,2,1824]{2,1,0:T(2,128)(2,1)S(1)}, u32[]{:S(2)}, u32[]{:S(2)}) async-start(bf16[64,2,1824]{2,1,0:T(2,128)(2,1)} %reshape.729), calls=%async_computation.1 | async-start | bytes 983040 | tf_op jit(solution)/shard_map/all_to_all | solution.py:39
  79.8 29.9 %copy-start.24 = (s32[128]{0:T(128)}, s32[128]{0:T(128)S(1)}, u32[]{:S(2)}) copy-start(s32[128]{0:T(128)S(1)} %iota_add_fusion) | copy-start | bytes 1540
  98.3 7.4 %copy-start.3 = (bf16[64,1,3648]{2,0,1:T(8,128)(2,1)}, bf16[64,1,3648]{2,0,1:T(8,128)(2,1)S(1)}, u32[]{:S(2)}) copy-start(bf16[64,1,3648]{2,0,1:T(8,128)(2,1)S(1)} %copy.203) | copy-start | bytes 1400836
  105.7 2.7 copy-start.5
  105.7 2.7 copy-start.11
  107.8 1.2 copy-start.1
  108.4 1.2 copy-start.4
  108.5 1.2 copy-start.26
  108.5 1.2 copy-start.29
  109.7 1.5 copy-start.8
  111.1 1.4 copy-start.19
  117.9 5.1 %copy-start.7 = (bf16[128,576]{0,1:T(8,128)(2,1)S(1)}, bf16[128,576]{0,1:T(8,128)(2,1)}, u32[]{:S(2)}) copy-start(bf16[128,576]{0,1:T(8,128)(2,1)} %get-tuple-element.41) | copy-start | bytes 442372
  117.9 5.1 %copy-start.23 = (pred[1024]{0:T(1024)(128)(4,1)S(1)}, pred[1024]{0:T(1024)(128)(4,1)}, u32[]{:S(2)}) copy-start(pred[1024]{0:T(1024)(128)(4,1)} %eq.125) | copy-start | bytes 3076
  117.9 5.1 %copy-start.25 = (s32[128]{0:T(128)S(1)}, s32[128]{0:T(128)}, u32[]{:S(2)}) copy-start(s32[128]{0:T(128)} %copy-done.24) | copy-start | bytes 1540
  119.9 5.1 %copy-start.6 = (bf16[128,576]{0,1:T(8,128)(2,1)S(1)}, bf16[128,576]{0,1:T(8,128)(2,1)}, u32[]{:S(2)}) copy-start(bf16[128,576]{0,1:T(8,128)(2,1)} %get-tuple-element.42) | copy-start | bytes 442372
  119.9 5.1 %copy-start.9 = (f32[1024,128]{0,1:T(8,128)S(1)}, f32[1024,128]{0,1:T(8,128)}, u32[]{:S(2)}) copy-start(f32[1024,128]{0,1:T(8,128)} %copy-done.8) | copy-start | bytes 1572868
  119.9 5.1 %copy-start.20 = (f32[1024]{0:T(1024)S(1)}, f32[1024]{0:T(1024)}, u32[]{:S(2)}) copy-start(f32[1024]{0:T(1024)} %copy-done.19) | copy-start | bytes 12292
  119.9 5.1 %copy-start.27 = (pred[1024]{0:T(1024)(128)(4,1)S(1)}, pred[1024]{0:T(1024)(128)(4,1)}, u32[]{:S(2)}) copy-start(pred[1024]{0:T(1024)(128)(4,1)} %eq.122) | copy-start | bytes 3076
  123.0 4.0 copy-start.21
  124.9 2.0 copy-start.22
  124.9 2.2 copy-start.31
  124.9 2.2 copy-start.30
  124.9 2.3 copy-start.12
  124.9 2.3 copy-start.13
  124.9 2.3 copy-start.14
  125.0 2.3 copy-start.15
  125.0 2.3 copy-start.32
  125.0 2.3 copy-start.33
  125.0 2.3 copy-start.34
  125.0 2.3 copy-start.35
  131.3 4.3 copy-start.2
  137.5 67.9 %all-to-all-start.2 = ((f32[64,16,514]{2,1,0:T(8,128)}), f32[64,16,514]{2,1,0:T(8,128)}, u32[]{:S(2)}, u32[]{:S(2)}) async-start(f32[64,16,514]{2,1,0:T(8,128)} %pad_maximum_fusion), calls=%async_computation.2 | async-start | bytes 5242880 | tf_op jit(solution)/shard_map/all_to_all | solution.py:39
  143.7 171.6 %all-gather.9.cloned.1.call-start = ((), (), s32[]{:S(2)}) async-start(), calls=%async_computation.12 | async-start | bytes 1310720 | tf_op jit(solution)/shard_map/all_gather | solution.py:178
  145.0 1.1 copy-start.18
  209.8 33.1 %copy-start.16 = (bf16[32,2048]{1,0:T(8,128)(2,1)S(1)}, bf16[32,2048]{1,0:T(8,128)(2,1)}, u32[]{:S(2)}) copy-start(bf16[32,2048]{1,0:T(8,128)(2,1)} %param.26) | copy-start | bytes 393220
  214.8 52.3 %copy-start.28 = (f32[2048]{0:T(1024)S(1)}, f32[2048]{0:T(1024)}, u32[]{:S(2)}) copy-start(f32[2048]{0:T(1024)} %param.27) | copy-start | bytes 24580
  267.1 26.5 %copy-start.17 = (s32[64,4,6]{0,1,2:T(4,128)S(1)}, s32[64,4,6]{0,1,2:T(4,128)}, u32[]{:S(2)}) copy-start(s32[64,4,6]{0,1,2:T(4,128)} %param.29) | copy-start | bytes 18436
  292.8 107.9 %all-gather.7.cloned.1.call-start = ((), (), s32[]{:S(2)}) async-start(), calls=%async_computation.10 | async-start | bytes 6389760 | tf_op jit(solution)/shard_map/all_gather | solution.py:81
  293.6 140.1 %reduce-scatter.2.cloned.1.call-start = ((), (), s32[]{:S(2)}) async-start(), calls=%async_computation.11 | async-start | bytes 1310720 | tf_op jit(solution)/shard_map/reduce_scatter | solution.py:212
  336.9 69.5 %copy-start.39 = (bf16[704,32]{0,1:T(8,128)(2,1)S(1)}, bf16[704,32]{0,1:T(8,128)(2,1)}, u32[]{:S(2)}) copy-start(bf16[704,32]{0,1:T(8,128)(2,1)} %param.33) | copy-start | bytes 135172
Sparse Core Ops, SparseCore 0:
  10.1 88.1 all-gather.4
  292.9 22.4 all-gather.8
  318.2 82.4 all-gather.6
  412.3 21.3 reduce-scatter.1
